TPU v7x, 128 devices: a whole 4x4x4 slice. The times are simulated.
128 devices in a mesh: src: 16 (over y_lo, z, core), tgt: 8 (over y_hi, x).
Axes of the slice: x: 4, y: 4 (y_hi: 2, y_lo: 2; y = y_hi * 2 + y_lo), z: 4, core: 2. Of those that a mesh axis runs over, the one named last changes fastest.
Arguments:
- src_emb: bfloat16 [16384, 768], P(('src', 'tgt')), may hold values from -0.05119037 to 0.05119037
- right_sentence_vectors: bfloat16 [8192, 768], P(('tgt', 'src')), may hold values from -0.05119037 to 0.05119037
- src_mass: float32 [16384], P('src'), may hold values from 0.25 to 4
- tgt_mass: float32 [8192], P('tgt'), may hold values from 0.5 to 8
Outputs:
- grad_src: float32 [16384, 768], P(('src', 'tgt'))
- grad_tgt: float32 [8192, 768], P(('tgt', 'src'))
All inputs are finite; a program needn't handle non-finite values.
Results may differ from a plain program's by a relative error of at most 0.00045.
Values may be sent and summed in bfloat16 or wider, within the bound.
No kernel may reach another device: no remote copies, remote signals or barrier semaphores. Data moves between devices by JAX's collectives and lax.ppermute only.
A program may use at most 64 MiB of HBM per device.

v0:
```python
import jax
import jax.numpy as jnp
from jax import lax
from jax.sharding import PartitionSpec as P

ITERS = 4
regularizer_epsilon = 0.05
highest = lax.Precision.HIGHEST


def row_total(part):
    return lax.psum(part, "tgt")


def col_total(part):
    return lax.psum(part, "src")


def times_vector(kernel, vector):
    return jnp.dot(kernel, vector, precision=highest, preferred_element_type=jnp.float32)


def vector_times(vector, kernel):
    return jnp.dot(vector, kernel, precision=highest, preferred_element_type=jnp.float32)


def per_device(src_emb, right_sentence_vectors, src_mass, tgt_mass):
    src_rows = lax.all_gather(src_emb, "tgt", axis=0, tiled=True)
    target_rows = lax.all_gather(right_sentence_vectors, "src", axis=0, tiled=True)

    def build():
        kernel_grid = (
            lax.dot_general(
                src_rows, target_rows, (((1,), (1,)), ((), ())), preferred_element_type=jnp.float32
            )
            / regularizer_epsilon
        )
        kernel = lax.optimization_barrier(jnp.exp(kernel_grid).astype(jnp.bfloat16))
        return (kernel_grid, kernel)

    kernel_grid, kernel = build()
    vector = jnp.ones(tgt_mass.shape, jnp.float32)
    old_saved, row_saved, src_saved, col_saved, tgt_saved = ([], [], [], [], [])
    for iteration in range(ITERS):
        old_saved.append(vector)
        row_sum = row_total(times_vector(kernel, vector))
        src_scale = src_mass / row_sum
        col_sum = col_total(vector_times(src_scale, kernel))
        vector = tgt_mass / col_sum
        row_saved.append(row_sum)
        src_saved.append(src_scale)
        col_saved.append(col_sum)
        tgt_saved.append(vector)
    last_src = src_saved[-1]
    last_tgt = tgt_saved[-1]
    weighted = kernel * kernel_grid
    src_adj = row_total(times_vector(weighted, last_tgt))
    tgt_adj = col_total(vector_times(last_src, weighted))
    row_bars = [None] * ITERS
    col_bars = [None] * ITERS
    for iteration in reversed(range(ITERS)):
        kernel_grid, kernel = build()
        col_bar = -tgt_adj * tgt_saved[iteration] / col_saved[iteration]
        back = row_total(times_vector(kernel, col_bar))
        if iteration == ITERS - 1:
            back = back + src_adj
        row_bar = -back * src_saved[iteration] / row_saved[iteration]
        if iteration > 0:
            tgt_adj = col_total(vector_times(row_bar, kernel))
        row_bars[iteration] = row_bar
        col_bars[iteration] = col_bar
    left = jnp.stack(row_bars + src_saved, axis=1)
    right = jnp.stack(old_saved + col_bars, axis=1)
    lowrank = lax.dot_general(
        left, right, (((1,), (1,)), ((), ())), precision=highest, preferred_element_type=jnp.float32
    )
    cross_term_grid = (
        kernel * (last_src[:, None] * last_tgt[None, :] * (1.0 + kernel_grid) + lowrank)
    ).astype(jnp.bfloat16)
    left_share_piece = (
        jnp.dot(cross_term_grid, target_rows, preferred_element_type=jnp.float32)
        / regularizer_epsilon
    )
    right_share_piece = (
        lax.dot_general(
            cross_term_grid, src_rows, (((0,), (0,)), ((), ())), preferred_element_type=jnp.float32
        )
        / regularizer_epsilon
    )
    src_whole = lax.psum(left_share_piece, "tgt")
    tgt_whole = lax.psum(right_share_piece, "src")
    src_count = src_emb.shape[0]
    tgt_count = right_sentence_vectors.shape[0]
    grad_src = lax.dynamic_slice_in_dim(src_whole, lax.axis_index("tgt") * src_count, src_count, 0)
    grad_tgt = lax.dynamic_slice_in_dim(tgt_whole, lax.axis_index("src") * tgt_count, tgt_count, 0)
    return (grad_src, grad_tgt)


def solution(mesh):
    placed = (P(("src", "tgt"), None), P(("tgt", "src"), None), P("src"), P("tgt"))
    return jax.shard_map(
        per_device,
        mesh=mesh,
        in_specs=placed,
        out_specs=(P(("src", "tgt"), None), P(("tgt", "src"), None)),
        check_vma=False,
    )
```

profile of v0, /device:TPU:1, one launch (start us, length us, event | category | flops | bytes accessed | tf_op | source)
XLA Modules:
  0.0 730.8 jit_solution(13594640266932629747)
XLA Ops:
  8.7 54.5 %all-gather.3.cloned.1.call-done = bf16[1024,768]{1,0:T(8,128)(2,1)} async-done(((bf16[128,768]{1,0:T(8,128)(2,1)}), bf16[1024,768]{1,0:T(8,128)(2,1)}) %all-gather.3.cloned.1.call-update) | async-done | bytes 1572880 | tf_op jit(solution)/shard_map/all_gather | solution.py:28
  63.2 35.8 %all-gather.5.cloned.1.call-done = bf16[1024,768]{1,0:T(8,128)(2,1)} async-done(((bf16[64,768]{1,0:T(8,128)(2,1)}), bf16[1024,768]{1,0:T(8,128)(2,1)}) %all-gather.5.cloned.1.call-update) | async-done | bytes 1572880 | tf_op jit(solution)/shard_map/all_gather | solution.py:29
  99.0 5.6 exponential_convert_fusion
  106.4 20.2 %psum.133 = f32[1024]{0:T(1024)S(1)} all-reduce(f32[1024]{0:T(1024)S(1)} %bitcast.122), channel_id=1, replica_groups=mesh['src'=16,'tgt'=8] {'tgt'}, use_global_device_ids=true, to_apply=%region_0.0 | all-reduce | flops 1024 | bytes 8192 | tf_op jit(solution)/shard_map/psum | solution.py:12
  127.5 30.5 %psum.134 = f32[1024]{0:T(1024)S(1)} all-reduce(f32[1024]{0:T(1024)S(1)} %bitcast.123), channel_id=1, replica_groups=mesh['src'=16,'tgt'=8] {'src'}, use_global_device_ids=true, to_apply=%region_1.0 | all-reduce | flops 1024 | bytes 8192 | tf_op jit(solution)/shard_map/psum | solution.py:16
  159.7 15.5 %psum.135 = f32[1024]{0:T(1024)S(1)} all-reduce(f32[1024]{0:T(1024)S(1)} %bitcast.124), channel_id=1, replica_groups=mesh['src'=16,'tgt'=8] {'tgt'}, use_global_device_ids=true, to_apply=%region_2.0 | all-reduce | flops 1024 | bytes 8192 | tf_op jit(solution)/shard_map/psum | solution.py:12
  176.2 30.6 %psum.136 = f32[1024]{0:T(1024)S(1)} all-reduce(f32[1024]{0:T(1024)S(1)} %bitcast.125), channel_id=1, replica_groups=mesh['src'=16,'tgt'=8] {'src'}, use_global_device_ids=true, to_apply=%region_3.0 | all-reduce | flops 1024 | bytes 8192 | tf_op jit(solution)/shard_map/psum | solution.py:16
  208.5 17.2 %psum.137 = f32[1024]{0:T(1024)S(1)} all-reduce(f32[1024]{0:T(1024)S(1)} %bitcast.126), channel_id=1, replica_groups=mesh['src'=16,'tgt'=8] {'tgt'}, use_global_device_ids=true, to_apply=%region_4.0 | all-reduce | flops 1024 | bytes 8192 | tf_op jit(solution)/shard_map/psum | solution.py:12
  226.6 30.9 %psum.138 = f32[1024]{0:T(1024)S(1)} all-reduce(f32[1024]{0:T(1024)S(1)} %bitcast.127), channel_id=1, replica_groups=mesh['src'=16,'tgt'=8] {'src'}, use_global_device_ids=true, to_apply=%region_5.0 | all-reduce | flops 1024 | bytes 8192 | tf_op jit(solution)/shard_map/psum | solution.py:16
  259.3 15.6 %psum.139 = f32[1024]{0:T(1024)S(1)} all-reduce(f32[1024]{0:T(1024)S(1)} %bitcast.128), channel_id=1, replica_groups=mesh['src'=16,'tgt'=8] {'tgt'}, use_global_device_ids=true, to_apply=%region_6.0 | all-reduce | flops 1024 | bytes 8192 | tf_op jit(solution)/shard_map/psum | solution.py:12
  275.8 4.6 fusion.2
  280.5 31.1 %all-reduce = (f32[1024]{0:T(1024)S(1)}, f32[1024]{0:T(1024)S(1)}) all-reduce(f32[1024]{0:T(1024)S(1)} %bitcast.120, f32[1024]{0:T(1024)S(1)} %bitcast.121), channel_id=1, replica_groups=mesh['src'=16,'tgt'=8] {'src'}, use_global_device_ids=true, to_apply=%region_7.0 | all-reduce | flops 2048 | bytes 16384 | tf_op jit(solution)/shard_map/psum | solution.py:16
  311.6 6.1 fusion.1
  319.4 17.2 %psum.152 = f32[1024]{0:T(1024)S(1)} all-reduce(f32[1024]{0:T(1024)S(1)} %add.58), channel_id=1, replica_groups=mesh['src'=16,'tgt'=8] {'tgt'}, use_global_device_ids=true, to_apply=%region_9.0 | all-reduce | flops 1024 | bytes 8192 | tf_op jit(solution)/shard_map/psum | solution.py:12
  337.6 30.9 %psum.144 = f32[1024]{0:T(1024)S(1)} all-reduce(f32[1024]{0:T(1024)S(1)} %bitcast.129), channel_id=1, replica_groups=mesh['src'=16,'tgt'=8] {'src'}, use_global_device_ids=true, to_apply=%region_11.0 | all-reduce | flops 1024 | bytes 8192 | tf_op jit(solution)/shard_map/psum | solution.py:16
  370.2 15.5 %psum.145 = f32[1024]{0:T(1024)S(1)} all-reduce(f32[1024]{0:T(1024)S(1)} %bitcast.130), channel_id=1, replica_groups=mesh['src'=16,'tgt'=8] {'tgt'}, use_global_device_ids=true, to_apply=%region_12.0 | all-reduce | flops 1024 | bytes 8192 | tf_op jit(solution)/shard_map/psum | solution.py:12
  386.7 30.6 %psum.146 = f32[1024]{0:T(1024)S(1)} all-reduce(f32[1024]{0:T(1024)S(1)} %bitcast.131), channel_id=1, replica_groups=mesh['src'=16,'tgt'=8] {'src'}, use_global_device_ids=true, to_apply=%region_13.0 | all-reduce | flops 1024 | bytes 8192 | tf_op jit(solution)/shard_map/psum | solution.py:16
  419.0 17.4 %psum.147 = f32[1024]{0:T(1024)S(1)} all-reduce(f32[1024]{0:T(1024)S(1)} %bitcast.132), channel_id=1, replica_groups=mesh['src'=16,'tgt'=8] {'tgt'}, use_global_device_ids=true, to_apply=%region_14.0 | all-reduce | flops 1024 | bytes 8192 | tf_op jit(solution)/shard_map/psum | solution.py:12
  437.4 30.9 %psum.148 = f32[1024]{0:T(1024)S(1)} all-reduce(f32[1024]{0:T(1024)S(1)} %bitcast.133), channel_id=1, replica_groups=mesh['src'=16,'tgt'=8] {'src'}, use_global_device_ids=true, to_apply=%region_15.0 | all-reduce | flops 1024 | bytes 8192 | tf_op jit(solution)/shard_map/psum | solution.py:16
  470.1 15.5 %psum.149 = f32[1024]{0:T(1024)S(1)} all-reduce(f32[1024]{0:T(1024)S(1)} %bitcast.119), channel_id=1, replica_groups=mesh['src'=16,'tgt'=8] {'tgt'}, use_global_device_ids=true, to_apply=%region_16.0 | all-reduce | flops 1024 | bytes 8192 | tf_op jit(solution)/shard_map/psum | solution.py:12
  485.7 6.2 fusion
  498.3 5.0 convolution_multiply_fusion
  503.3 88.4 %all-reduce.4.cloned.1.call-done = f32[1024,768]{1,0:T(8,128)} async-done(((f32[1024,768]{1,0:T(8,128)}), f32[1024,768]{1,0:T(8,128)}) %all-reduce.4.cloned.1.call-update) | async-done | bytes 3145744 | tf_op jit(solution)/shard_map/psum | solution.py:90
  593.5 129.1 %all-reduce.6.cloned.1.call-done = f32[1024,768]{1,0:T(8,128)} async-done(((f32[1024,768]{1,0:T(8,128)}), f32[1024,768]{1,0:T(8,128)}) %all-reduce.6.cloned.1.call-update) | async-done | bytes 3145744 | tf_op jit(solution)/shard_map/psum | solution.py:91
  (55 shorter events, 31.8 us)
Async XLA Ops:
  7.2 56.0 %all-gather.3.cloned.1.call-start = ((), (), s32[]{:S(2)}) async-start(), calls=%async_computation | async-start | bytes 1769472 | tf_op jit(solution)/shard_map/all_gather | solution.py:28
  7.9 91.1 %all-gather.5.cloned.1.call-start = ((), (), s32[]{:S(2)}) async-start(), calls=%async_computation.1 | async-start | bytes 1671168 | tf_op jit(solution)/shard_map/all_gather | solution.py:29
  8.6 583.1 %all-reduce.4.cloned.1.call-start = ((), (), s32[]{:S(2)}) async-start(), calls=%async_computation.2 | async-start | bytes 6291456 | tf_op jit(solution)/shard_map/psum | solution.py:90
  104.6 21.9 %copy-start.2 = (f32[1024]{0:T(1024)S(1)}, f32[1024]{0:T(1024)}, u32[]{:S(2)}) copy-start(f32[1024]{0:T(1024)} %param.6) | copy-start | bytes 12292
  104.6 53.4 %copy-start.3 = (f32[1024]{0:T(1024)S(1)}, f32[1024]{0:T(1024)}, u32[]{:S(2)}) copy-start(f32[1024]{0:T(1024)} %param.7) | copy-start | bytes 12292
  485.6 7.6 %copy-start.4 = (bf16[1024,768]{1,0:T(8,128)(2,1)S(1)}, bf16[1024,768]{1,0:T(8,128)(2,1)}, u32[]{:S(2)}) copy-start(bf16[1024,768]{1,0:T(8,128)(2,1)} %all-gather.5.cloned.1.call-done) | copy-start | bytes 4718596
  491.9 1.3 copy-start
  496.7 1.6 copy-start.1
  496.8 225.9 %all-reduce.6.cloned.1.call-start = ((), (), s32[]{:S(2)}) async-start(), calls=%async_computation.3 | async-start | bytes 6291456 | tf_op jit(solution)/shard_map/psum | solution.py:91
Sparse Core Ops, SparseCore 0:
  10.3 52.8 all-gather.2
  64.9 34.0 all-gather.4
  496.9 94.8 all-reduce.3
  594.1 128.4 all-reduce.5
where the time goes:
time: 731 us
  blocking collectives  350 us (48%)
  waiting for transfers between devices  309 us (42%)
  matrix products  51.4 us (7%)
  between operations  13.9 us (2%)
    psum x7, blocking collectives, col_total(): return lax.psum(part, 'src')  216 us
    psum x8, blocking collectives, row_total(): return lax.psum(part, 'tgt')  134 us
    psum x1, waiting for transfers between devices, per_device(): tgt_whole = lax.psum(right_share_piece, 'src')  129 us
    psum x1, waiting for transfers between devices, per_device(): src_whole = lax.psum(left_share_piece, 'tgt')  88.4 us
    all_gather x1, waiting for transfers between devices, per_device(): src_rows = lax.all_gather(src_emb, 'tgt', axis=0, tiled=True)  54.5 us
    all_gather x1, waiting for transfers between devices, per_device(): lax.all_gather(right_sentence_vectors, 'src', axis=0, tiled=True)  35.8 us
    dot_general x9, matrix products, times_vector(): jnp.dot(kernel, vector, precision=highest, preferred_element_type=jnp.flo...  19.9 us
  transfers between devices with their start and end apart: 4, of which 4 were waited for; matrix products, arithmetic and copies ran while one was open for 1% of the time, Pallas kernels for 0%

commit v1 on v0

--- a/solution.py
+++ b/solution.py
@@ -13,7 +13,7 @@
 
 
 def col_total(part):
-    return lax.psum(part, "src")
+    return jnp.sum(lax.all_gather(part, "src"), axis=0)
 
 
 def times_vector(kernel, vector):

time: 731 us -> 680 us (0.930)
  blocking collectives: 350 us -> 298 us
    psum x7 -> x0, blocking collectives: 216 us -> none  [col_total(): return lax.psum(part, 'src')]
    all_gather x0 -> x8, blocking collectives: none -> 162 us  [col_total(): return jnp.sum(lax.all_gather(part, 'src'), axis=0)]
where the time goes in v1:
time: 680 us
  waiting for transfers between devices  309 us (45%)
  blocking collectives  298 us (44%)
  matrix products  51.3 us (8%)
  between operations  14 us (2%)
    all_gather x8, blocking collectives, col_total(): return jnp.sum(lax.all_gather(part, 'src'), axis=0)  162 us
    psum x8, blocking collectives, row_total(): return lax.psum(part, 'tgt')  136 us
    psum x1, waiting for transfers between devices, per_device(): tgt_whole = lax.psum(right_share_piece, 'src')  129 us
    psum x1, waiting for transfers between devices, per_device(): src_whole = lax.psum(left_share_piece, 'tgt')  88.6 us
    all_gather x1, waiting for transfers between devices, per_device(): src_rows = lax.all_gather(src_emb, 'tgt', axis=0, tiled=True)  54.5 us
    all_gather x1, waiting for transfers between devices, per_device(): lax.all_gather(right_sentence_vectors, 'src', axis=0, tiled=True)  35.8 us
    dot_general x9, matrix products, times_vector(): jnp.dot(kernel, vector, precision=highest, preferred_element_type=jnp.flo...  19.9 us
  transfers between devices with their start and end apart: 4, of which 4 were waited for; matrix products, arithmetic and copies ran while one was open for 1% of the time, Pallas kernels for 0%

profile of v1, /device:TPU:1, one launch (start us, length us, event | category | flops | bytes accessed | tf_op | source)
XLA Modules:
  0.0 679.6 jit_solution(10737722344350064251)
XLA Ops:
  8.7 54.5 %all-gather.11.cloned.1.call-done = bf16[1024,768]{1,0:T(8,128)(2,1)} async-done(((bf16[128,768]{1,0:T(8,128)(2,1)}), bf16[1024,768]{1,0:T(8,128)(2,1)}) %all-gather.11.cloned.1.call-update) | async-done | bytes 1572880 | tf_op jit(solution)/shard_map/all_gather | solution.py:28
  63.2 35.8 %all-gather.13.cloned.1.call-done = bf16[1024,768]{1,0:T(8,128)(2,1)} async-done(((bf16[64,768]{1,0:T(8,128)(2,1)}), bf16[1024,768]{1,0:T(8,128)(2,1)}) %all-gather.13.cloned.1.call-update) | async-done | bytes 1572880 | tf_op jit(solution)/shard_map/all_gather | solution.py:29
  99.0 5.6 exponential_convert_fusion
  106.4 20.2 %psum.77 = f32[1024]{0:T(1024)S(1)} all-reduce(f32[1024]{0:T(1024)S(1)} %bitcast.128), channel_id=1, replica_groups=mesh['src'=16,'tgt'=8] {'tgt'}, use_global_device_ids=true, to_apply=%region_0.0 | all-reduce | flops 1024 | bytes 8192 | tf_op jit(solution)/shard_map/psum | solution.py:12
  127.5 21.3 %all-gather = f32[16384]{0:T(1024)S(1)} all-gather(f32[1024]{0:T(1024)S(1)} %bitcast.120), channel_id=2, replica_groups=mesh['src'=16,'tgt'=8] {'src'}, dimensions={0}, use_global_device_ids=true | all-gather | bytes 69632 | tf_op jit(solution)/shard_map/all_gather | solution.py:16
  150.6 15.5 %psum.78 = f32[1024]{0:T(1024)S(1)} all-reduce(f32[1024]{0:T(1024)S(1)} %bitcast.129), channel_id=1, replica_groups=mesh['src'=16,'tgt'=8] {'tgt'}, use_global_device_ids=true, to_apply=%region_2.0 | all-reduce | flops 1024 | bytes 8192 | tf_op jit(solution)/shard_map/psum | solution.py:12
  167.1 20.1 %all-gather.1 = f32[16384]{0:T(1024)S(1)} all-gather(f32[1024]{0:T(1024)S(1)} %bitcast.121), channel_id=3, replica_groups=mesh['src'=16,'tgt'=8] {'src'}, dimensions={0}, use_global_device_ids=true | all-gather | bytes 69632 | tf_op jit(solution)/shard_map/all_gather | solution.py:16
  189.0 17.8 %psum.79 = f32[1024]{0:T(1024)S(1)} all-reduce(f32[1024]{0:T(1024)S(1)} %bitcast.130), channel_id=1, replica_groups=mesh['src'=16,'tgt'=8] {'tgt'}, use_global_device_ids=true, to_apply=%region_4.0 | all-reduce | flops 1024 | bytes 8192 | tf_op jit(solution)/shard_map/psum | solution.py:12
  207.7 20.6 %all-gather.2 = f32[16384]{0:T(1024)S(1)} all-gather(f32[1024]{0:T(1024)S(1)} %bitcast.122), channel_id=4, replica_groups=mesh['src'=16,'tgt'=8] {'src'}, dimensions={0}, use_global_device_ids=true | all-gather | bytes 69632 | tf_op jit(solution)/shard_map/all_gather | solution.py:16
  230.1 16.4 %psum.80 = f32[1024]{0:T(1024)S(1)} all-reduce(f32[1024]{0:T(1024)S(1)} %bitcast.131), channel_id=1, replica_groups=mesh['src'=16,'tgt'=8] {'tgt'}, use_global_device_ids=true, to_apply=%region_6.0 | all-reduce | flops 1024 | bytes 8192 | tf_op jit(solution)/shard_map/psum | solution.py:12
  252.1 20.0 %all-gather.4 = f32[16384]{0:T(1024)S(1)} all-gather(f32[1024]{0:T(1024)S(1)} %bitcast.123), channel_id=6, replica_groups=mesh['src'=16,'tgt'=8] {'src'}, dimensions={0}, use_global_device_ids=true | all-gather | bytes 69632 | tf_op jit(solution)/shard_map/all_gather | solution.py:16
  272.2 17.8 %all-gather.3 = f32[16384]{0:T(1024)S(1)} all-gather(f32[1024]{0:T(1024)S(1)} %bitcast.117), channel_id=5, replica_groups=mesh['src'=16,'tgt'=8] {'src'}, dimensions={0}, use_global_device_ids=true | all-gather | bytes 69632 | tf_op jit(solution)/shard_map/all_gather | solution.py:16
  290.0 6.1 fusion.1
  297.9 17.1 %psum.88 = f32[1024]{0:T(1024)S(1)} all-reduce(f32[1024]{0:T(1024)S(1)} %add.42), channel_id=1, replica_groups=mesh['src'=16,'tgt'=8] {'tgt'}, use_global_device_ids=true, to_apply=%region_9.0 | all-reduce | flops 1024 | bytes 8192 | tf_op jit(solution)/shard_map/psum | solution.py:12
  316.0 20.8 %all-gather.5 = f32[16384]{0:T(1024)S(1)} all-gather(f32[1024]{0:T(1024)S(1)} %bitcast.124), channel_id=7, replica_groups=mesh['src'=16,'tgt'=8] {'src'}, dimensions={0}, use_global_device_ids=true | all-gather | bytes 69632 | tf_op jit(solution)/shard_map/all_gather | solution.py:16
  338.6 15.5 %psum.83 = f32[1024]{0:T(1024)S(1)} all-reduce(f32[1024]{0:T(1024)S(1)} %bitcast.132), channel_id=1, replica_groups=mesh['src'=16,'tgt'=8] {'tgt'}, use_global_device_ids=true, to_apply=%region_12.0 | all-reduce | flops 1024 | bytes 8192 | tf_op jit(solution)/shard_map/psum | solution.py:12
  355.0 20.9 %all-gather.6 = f32[16384]{0:T(1024)S(1)} all-gather(f32[1024]{0:T(1024)S(1)} %bitcast.125), channel_id=8, replica_groups=mesh['src'=16,'tgt'=8] {'src'}, dimensions={0}, use_global_device_ids=true | all-gather | bytes 69632 | tf_op jit(solution)/shard_map/all_gather | solution.py:16
  377.7 17.7 %psum.84 = f32[1024]{0:T(1024)S(1)} all-reduce(f32[1024]{0:T(1024)S(1)} %bitcast.133), channel_id=1, replica_groups=mesh['src'=16,'tgt'=8] {'tgt'}, use_global_device_ids=true, to_apply=%region_14.0 | all-reduce | flops 1024 | bytes 8192 | tf_op jit(solution)/shard_map/psum | solution.py:12
  396.3 20.2 %all-gather.7 = f32[16384]{0:T(1024)S(1)} all-gather(f32[1024]{0:T(1024)S(1)} %bitcast.126), channel_id=9, replica_groups=mesh['src'=16,'tgt'=8] {'src'}, dimensions={0}, use_global_device_ids=true | all-gather | bytes 69632 | tf_op jit(solution)/shard_map/all_gather | solution.py:16
  418.4 15.8 %psum.85 = f32[1024]{0:T(1024)S(1)} all-reduce(f32[1024]{0:T(1024)S(1)} %bitcast.127), channel_id=1, replica_groups=mesh['src'=16,'tgt'=8] {'tgt'}, use_global_device_ids=true, to_apply=%region_16.0 | all-reduce | flops 1024 | bytes 8192 | tf_op jit(solution)/shard_map/psum | solution.py:12
  434.3 6.2 fusion
  447.0 5.0 convolution_multiply_fusion
  452.0 88.6 %all-reduce.3.cloned.1.call-done = f32[1024,768]{1,0:T(8,128)} async-done(((f32[1024,768]{1,0:T(8,128)}), f32[1024,768]{1,0:T(8,128)}) %all-reduce.3.cloned.1.call-update) | async-done | bytes 3145744 | tf_op jit(solution)/shard_map/psum | solution.py:90
  542.3 129.1 %all-reduce.5.cloned.1.call-done = f32[1024,768]{1,0:T(8,128)} async-done(((f32[1024,768]{1,0:T(8,128)}), f32[1024,768]{1,0:T(8,128)}) %all-reduce.5.cloned.1.call-update) | async-done | bytes 3145744 | tf_op jit(solution)/shard_map/psum | solution.py:91
  (72 shorter events, 36.7 us)
Async XLA Ops:
  7.2 56.0 %all-gather.11.cloned.1.call-start = ((), (), s32[]{:S(2)}) async-start(), calls=%async_computation | async-start | bytes 1769472 | tf_op jit(solution)/shard_map/all_gather | solution.py:28
  7.9 91.1 %all-gather.13.cloned.1.call-start = ((), (), s32[]{:S(2)}) async-start(), calls=%async_computation.1 | async-start | bytes 1671168 | tf_op jit(solution)/shard_map/all_gather | solution.py:29
  8.6 531.9 %all-reduce.3.cloned.1.call-start = ((), (), s32[]{:S(2)}) async-start(), calls=%async_computation.2 | async-start | bytes 6291456 | tf_op jit(solution)/shard_map/psum | solution.py:90
  104.6 21.9 %copy-start.2 = (f32[1024]{0:T(1024)S(1)}, f32[1024]{0:T(1024)}, u32[]{:S(2)}) copy-start(f32[1024]{0:T(1024)} %param.6) | copy-start | bytes 12292
  104.6 44.2 %copy-start.3 = (f32[1024]{0:T(1024)S(1)}, f32[1024]{0:T(1024)}, u32[]{:S(2)}) copy-start(f32[1024]{0:T(1024)} %param.7) | copy-start | bytes 12292
  434.3 7.6 %copy-start.4 = (bf16[1024,768]{1,0:T(8,128)(2,1)S(1)}, bf16[1024,768]{1,0:T(8,128)(2,1)}, u32[]{:S(2)}) copy-start(bf16[1024,768]{1,0:T(8,128)(2,1)} %all-gather.13.cloned.1.call-done) | copy-start | bytes 4718596
  440.5 1.3 copy-start
  445.4 1.6 copy-start.1
  445.4 226.0 %all-reduce.5.cloned.1.call-start = ((), (), s32[]{:S(2)}) async-start(), calls=%async_computation.3 | async-start | bytes 6291456 | tf_op jit(solution)/shard_map/psum | solution.py:91
Sparse Core Ops, SparseCore 0:
  10.3 52.8 all-gather.10
  64.9 34.0 all-gather.12
  445.5 94.9 all-reduce.2
  542.9 128.4 all-reduce.4
